TPU v7x, 512 devices: a whole 4x8x8 slice. The times are simulated.
512 devices in a mesh: rev: 8 (over z_lo, x), bin: 64 (over y, z_hi, core).
Axes of the slice: x: 4, y: 8, z: 8 (z_hi: 4, z_lo: 2; z = z_hi * 2 + z_lo), core: 2. Of those that a mesh axis runs over, the one named last changes fastest.
Arguments:
- snapshots: float32 [8, 512, 3, 24, 8, 128], P('rev', 'bin'), may hold values from -6 to 6
- phase_index: int32 [8, 512], P('rev', 'bin'), may hold values from 0 to 255, as said below
Outputs:
- stress_terms: float32 [4, 6, 256, 24, 8, 128], P(None, None, 'bin', 'rev')
- mean_velocity: float32 [3, 256, 24, 8, 128], P(None, 'bin', 'rev')
Inputs may be any that keep to these rules, and one draw needn't show every extreme that they name: `phase_index`: the rows b * 8 to (b + 1) * 8 - 1 of a revolution shard name bins b * 4 to (b + 1) * 4 - 1 only, and each of these bins at least once.
All inputs are finite; a program needn't handle non-finite values.
Results may differ from a plain program's by a relative error of at most 0.00017.
Values sent between devices are 32-bit elements; how exact they have to be, the bound alone decides.
No kernel may reach another device: no remote copies, remote signals or barrier semaphores. Data moves between devices by JAX's collectives and lax.ppermute only.
A program may use at most 64 MiB of HBM per device.

v0:
```python
import jax
import jax.numpy as jnp
from jax import lax
from jax.sharding import PartitionSpec as P

PHASES = 256
viscosity = 0.2
stress_pairs = ((0, 0), (0, 1), (0, 2), (1, 1), (1, 2), (2, 2))


def padded_2(cells, sides, width):
    for axis, dim in sides:
        count = lax.axis_size(axis)
        head = lax.slice_in_dim(cells, 0, width, axis=dim)
        tail = lax.slice_in_dim(cells, cells.shape[dim] - width, cells.shape[dim], axis=dim)
        cells = jnp.concatenate(
            [
                lax.ppermute(tail, axis, [(i, (i + 1) % count) for i in range(count)]),
                cells,
                lax.ppermute(head, axis, [((i + 1) % count, i) for i in range(count)]),
            ],
            axis=dim,
        )
    return cells


def pair_index(first, second):
    low, high = (min(first, second), max(first, second))
    return stress_pairs.index((low, high))


def binned(frames, weights):
    vel_x, vel_y, vel_z = (frames[:, 0], frames[:, 1], frames[:, 2])
    stacked = jnp.stack(
        [
            jnp.ones_like(vel_x),
            vel_x,
            vel_y,
            vel_z,
            vel_x * vel_x,
            vel_x * vel_y,
            vel_x * vel_z,
            vel_y * vel_y,
            vel_y * vel_z,
            vel_z * vel_z,
        ],
        axis=1,
    )
    return jnp.einsum("ps,sfxyz->xfpyz", weights, stacked, precision=lax.Precision.HIGHEST)


def first_diff(shifted):
    return (
        0.75 * (shifted(1) - shifted(-1))
        - 0.15 * (shifted(2) - shifted(-2))
        + (shifted(3) - shifted(-3)) / 60.0
    )


def second_diff(shifted, centre):
    return (
        -49.0 / 18.0 * centre
        + 1.5 * (shifted(1) + shifted(-1))
        - 0.15 * (shifted(2) + shifted(-2))
        + (shifted(3) + shifted(-3)) / 90.0
    )


def finish_terms(owned):
    planes, bins_dev = (owned.shape[0], owned.shape[2])
    samples = owned[:, 0]
    velocity = [owned[:, 1 + comp] / samples for comp in range(3)]
    stresses = [
        owned[:, 4 + slot] / samples - velocity[pair[0]] * velocity[pair[1]]
        for slot, pair in enumerate(stress_pairs)
    ]
    fields = jnp.stack(velocity + stresses, axis=1)
    padded = padded_2(fields, (("rev", 0), ("bin", 2)), 3)

    def along(component, dim, centre):
        source = padded[:, component]
        if dim == 0:
            return lambda amount: source[3 + amount : 3 + amount + planes, 3 : 3 + bins_dev]
        if dim == 3:
            return lambda amount: source[3 : 3 + planes, 3 + amount : 3 + amount + bins_dev]
        return lambda amount: jnp.roll(centre, -amount, dim + 1)

    grad_u = [
        [first_diff(along(comp, dim, velocity[comp])) for dim in range(3)] for comp in range(3)
    ]
    unsteady, convect, produce, diffuse = ([], [], [], [])
    for slot, pair in enumerate(stress_pairs):
        first, second = pair
        stress = stresses[slot]
        unsteady.append(first_diff(along(3 + slot, 3, stress)))
        grads = [first_diff(along(3 + slot, dim, stress)) for dim in range(3)]
        convect.append(velocity[0] * grads[0] + velocity[1] * grads[1] + velocity[2] * grads[2])
        summed = jnp.zeros_like(stress)
        for dim in range(3):
            summed = (
                summed
                + stresses[pair_index(first, dim)] * grad_u[second][dim]
                + stresses[pair_index(second, dim)] * grad_u[first][dim]
            )
        produce.append(-summed)
        diffuse.append(
            viscosity
            * (
                second_diff(along(3 + slot, 0, stress), stress)
                + second_diff(along(3 + slot, 1, stress), stress)
                + second_diff(along(3 + slot, 2, stress), stress)
            )
        )
    terms_all = jnp.stack(
        [jnp.stack(unsteady), jnp.stack(convect), jnp.stack(produce), jnp.stack(diffuse)]
    )
    return (
        jnp.transpose(terms_all, (0, 1, 3, 2, 4, 5)),
        jnp.transpose(jnp.stack(velocity), (0, 2, 1, 3, 4)),
    )


def shards(snapshots, phase_index):
    frames = snapshots[0]
    bins_dev = PHASES // lax.axis_size("bin")
    planes = frames.shape[2] // lax.axis_size("rev")
    local_bins = phase_index[0] - lax.axis_index("bin") * bins_dev
    one_hot = (local_bins[None, :] == jnp.arange(bins_dev, dtype=jnp.int32)[:, None]).astype(
        jnp.float32
    )
    summed = lax.psum(binned(frames, one_hot), "rev")
    owned = lax.dynamic_slice_in_dim(summed, lax.axis_index("rev") * planes, planes, 0)
    return finish_terms(owned)


def solution(mesh):
    in_specs = (P("rev", "bin", None, None, None, None), P("rev", "bin"))
    out_specs = (P(None, None, "bin", "rev", None, None), P(None, "bin", "rev", None, None))
    return jax.shard_map(shards, mesh=mesh, in_specs=in_specs, out_specs=out_specs, check_vma=False)
```

profile of v0, /device:TPU:31, one launch (start us, length us, event | category | flops | bytes accessed | tf_op | source)
XLA Modules:
  0.0 230.9 jit_solution(12959993338759327280)
XLA Ops:
  7.2 1.0 broadcast_dynamic-update-slice_fusion
  8.2 3.0 %copy.18 = f32[1,8,3,24,8,128]{5,1,4,3,2,0:T(8,128)S(1)} copy(f32[1,8,3,24,8,128]{5,4,3,2,1,0:T(8,128)} %param.2) | data formatting | bytes 4718592 | tf_op args[0]
  11.2 2.8 %constant_dynamic-update-slice_fusion = f32[8,10,24,8,128]{4,0,3,2,1:T(8,128)} fusion(f32[8,10,24,8,128]{4,0,3,2,1:T(8,128)} %broadcast_dynamic-update-slice_fusion, f32[1,8,3,24,8,128]{5,4,3,2,1,0:T(8,128)S(1)} %copy-done), kind=kLoop, calls=%fused_computation.22 | loop fusion | bytes 4718592
  14.0 0.9 multiply_dynamic-update-slice_fusion.5
  15.0 1.0 multiply_dynamic-update-slice_fusion.4
  16.0 1.0 multiply_dynamic-update-slice_fusion.3
  17.0 0.9 multiply_dynamic-update-slice_fusion.2
  17.9 1.0 multiply_dynamic-update-slice_fusion.1
  18.9 1.0 multiply_dynamic-update-slice_fusion
  20.0 9.0 %convolution_bitcast_fusion = f32[24,10,4,8,128]{4,2,3,0,1:T(4,128)} fusion(f32[8,10,24,8,128]{4,0,3,2,1:T(8,128)} %multiply_dynamic-update-slice_fusion, s32[8]{0:T(128)S(1)} %subtract_bitcast_fusion), kind=kOutput, calls=%fused_computation.2 | convolution fusion | flops 94371872 | bytes 11796512 | tf_op jit(solution)/shard_map/ps,sfxyz->xfpyz/dot_general | solution.py:49
  29.0 113.4 %all-reduce.2.cloned.1.call-done = f32[24,10,4,8,128]{4,2,3,0,1:T(4,128)} async-done(((f32[24,10,4,8,128]{4,2,3,0,1:T(4,128)}), f32[24,10,4,8,128]{4,2,3,0,1:T(4,128)}) %all-reduce.2.cloned.1.call-update) | async-done | bytes 3932176 | tf_op jit(solution)/shard_map/psum | solution.py:131
  142.4 0.8 constant_dynamic-update-slice_fusion.9
  143.2 0.9 constant_dynamic-update-slice_fusion.8
  144.1 0.9 constant_dynamic-update-slice_fusion.7
  144.9 0.9 constant_dynamic-update-slice_fusion.6
  145.8 0.9 constant_dynamic-update-slice_fusion.5
  146.7 0.9 constant_dynamic-update-slice_fusion.4
  147.5 0.9 constant_dynamic-update-slice_fusion.3
  148.4 0.9 constant_dynamic-update-slice_fusion.2
  149.2 0.9 constant_dynamic-update-slice_fusion.1
  150.1 4.4 %collective-permute-start = (f32[3,9,4,8,128]{4,2,3,0,1:T(4,128)S(1)}, f32[3,9,4,8,128]{4,2,3,0,1:T(4,128)S(1)}, u32[]{:S(2)}, u32[]{:S(2)}) collective-permute-start(f32[3,9,4,8,128]{4,2,3,0,1:T(4,128)S(1)} %constant_dynamic-update-slice_fusion.1), channel_id=1, source_target_pairs={{0,64},{64,128},{128,192},{192,256},{256,320},{320,384},{384,448},... | collective-permute-start | bytes 1327112 | tf_op jit(solution)/shard_map/ppermute | solution.py:18
  154.5 1.9 collective-permute-start.1
  158.0 5.1 %collective-permute-done = f32[3,9,4,8,128]{4,2,3,0,1:T(4,128)S(1)} collective-permute-done((f32[3,9,4,8,128]{4,2,3,0,1:T(4,128)S(1)}, f32[3,9,4,8,128]{4,2,3,0,1:T(4,128)S(1)}, u32[]{:S(2)}, u32[]{:S(2)}) %collective-permute-start) | collective-permute-done | bytes 442400 | tf_op jit(solution)/shard_map/ppermute | solution.py:18
  163.2 5.9 %collective-permute-done.1 = f32[3,9,4,8,128]{4,2,3,0,1:T(4,128)S(1)} collective-permute-done((f32[3,9,4,8,128]{4,2,3,0,1:T(4,128)S(1)}, f32[3,9,4,8,128]{4,2,3,0,1:T(4,128)S(1)}, u32[]{:S(2)}, u32[]{:S(2)}) %collective-permute-start.1) | collective-permute-done | bytes 442400 | tf_op jit(solution)/shard_map/ppermute | solution.py:20
  169.1 0.3 pad_maximum_fusion.1
  169.4 0.8 fusion.99
  170.3 6.2 %collective-permute-start.2 = (f32[9,9,3,8,128]{4,3,2,1,0:T(8,128)S(1)}, f32[9,9,3,8,128]{4,3,2,1,0:T(8,128)S(1)}, u32[]{:S(2)}, u32[]{:S(2)}) collective-permute-start(f32[9,9,3,8,128]{4,3,2,1,0:T(8,128)S(1)} %copy.8), channel_id=1, source_target_pairs={{0,1},{1,2},{2,3},{3,4},{4,5},{5,6},{6,7},{7,8},{8,9},{9,10},{10,1... | collective-permute-start | bytes 2985992 | tf_op jit(solution)/shard_map/ppermute | solution.py:18
  176.7 2.1 collective-permute-start.3
  178.8 0.7 copy.13
  179.9 15.0 %collective-permute-done.2 = f32[9,9,3,8,128]{4,3,2,1,0:T(8,128)S(1)} collective-permute-done((f32[9,9,3,8,128]{4,3,2,1,0:T(8,128)S(1)}, f32[9,9,3,8,128]{4,3,2,1,0:T(8,128)S(1)}, u32[]{:S(2)}, u32[]{:S(2)}) %collective-permute-start.2) | collective-permute-done | bytes 995360 | tf_op jit(solution)/shard_map/ppermute | solution.py:18
  194.9 0.4 copy.10
  195.3 13.2 %collective-permute-done.3 = f32[9,9,3,8,128]{4,3,2,1,0:T(8,128)S(1)} collective-permute-done((f32[9,9,3,8,128]{4,3,2,1,0:T(8,128)S(1)}, f32[9,9,3,8,128]{4,3,2,1,0:T(8,128)S(1)}, u32[]{:S(2)}, u32[]{:S(2)}) %collective-permute-start.3) | collective-permute-done | bytes 995360 | tf_op jit(solution)/shard_map/ppermute | solution.py:20
  208.4 0.4 copy.11
  208.8 1.6 pad_maximum_fusion
  210.4 0.7 slice_bitcast_fusion.3
  211.0 1.3 constant_dynamic-update-slice_fusion.27
  213.8 1.3 constant_dynamic-update-slice_fusion.26
  216.0 1.2 constant_dynamic-update-slice_fusion.25
  218.9 0.3 constant_dynamic-update-slice_fusion.20
  219.6 0.3 constant_dynamic-update-slice_fusion.19
  220.3 0.3 constant_dynamic-update-slice_fusion.18
  220.7 0.3 constant_dynamic-update-slice_fusion.30
  221.1 0.3 constant_dynamic-update-slice_fusion.17
  221.4 0.3 constant_dynamic-update-slice_fusion.29
  221.8 0.3 constant_dynamic-update-slice_fusion.16
  222.2 0.3 constant_dynamic-update-slice_fusion.28
  222.5 0.4 maximum_bitcast_fusion
  222.9 1.1 copy.12
  (107 shorter events, 6.6 us)
Async XLA Ops:
  7.2 4.1 %copy-start = (f32[1,8,3,24,8,128]{5,4,3,2,1,0:T(8,128)S(1)}, f32[1,8,3,24,8,128]{5,4,3,2,1,0:T(8,128)}, u32[]{:S(2)}) copy-start(f32[1,8,3,24,8,128]{5,4,3,2,1,0:T(8,128)} %param.2) | copy-start | bytes 7077892
  7.2 135.2 %all-reduce.2.cloned.1.call-start = ((), (), s32[]{:S(2)}) async-start(), calls=%async_computation | async-start | bytes 7864320 | tf_op jit(solution)/shard_map/psum | solution.py:131
  16.0 4.0 %copy-start.1 = (s32[1,8]{1,0:T(1,128)S(1)}, s32[1,8]{1,0:T(1,128)}, u32[]{:S(2)}) copy-start(s32[1,8]{1,0:T(1,128)} %param.3) | copy-start | bytes 100
  150.1 13.1 %collective-permute-start = (f32[3,9,4,8,128]{4,2,3,0,1:T(4,128)S(1)}, f32[3,9,4,8,128]{4,2,3,0,1:T(4,128)S(1)}, u32[]{:S(2)}, u32[]{:S(2)}) collective-permute-start(f32[3,9,4,8,128]{4,2,3,0,1:T(4,128)S(1)} %constant_dynamic-update-slice_fusion.1), channel_id=1, source_target_pairs={{0,64},{64,128},{128,192},{192,256},{256,320},{320,384},{384,448},... | collective-permute-start | bytes 1327112 | tf_op jit(solution)/shard_map/ppermute | solution.py:18
  154.5 14.6 %collective-permute-start.1 = (f32[3,9,4,8,128]{4,2,3,0,1:T(4,128)S(1)}, f32[3,9,4,8,128]{4,2,3,0,1:T(4,128)S(1)}, u32[]{:S(2)}, u32[]{:S(2)}) collective-permute-start(f32[3,9,4,8,128]{4,2,3,0,1:T(4,128)S(1)} %constant_dynamic-update-slice_fusion.1), channel_id=1, source_target_pairs={{64,0},{128,64},{192,128},{256,192},{320,256},{384,320},{448,384},... | collective-permute-start | bytes 1327112 | tf_op jit(solution)/shard_map/ppermute | solution.py:20
  170.3 24.5 %collective-permute-start.2 = (f32[9,9,3,8,128]{4,3,2,1,0:T(8,128)S(1)}, f32[9,9,3,8,128]{4,3,2,1,0:T(8,128)S(1)}, u32[]{:S(2)}, u32[]{:S(2)}) collective-permute-start(f32[9,9,3,8,128]{4,3,2,1,0:T(8,128)S(1)} %copy.8), channel_id=1, source_target_pairs={{0,1},{1,2},{2,3},{3,4},{4,5},{5,6},{6,7},{7,8},{8,9},{9,10},{10,1... | collective-permute-start | bytes 2985992 | tf_op jit(solution)/shard_map/ppermute | solution.py:18
  176.7 31.8 %collective-permute-start.3 = (f32[9,9,3,8,128]{4,3,2,1,0:T(8,128)S(1)}, f32[9,9,3,8,128]{4,3,2,1,0:T(8,128)S(1)}, u32[]{:S(2)}, u32[]{:S(2)}) collective-permute-start(f32[9,9,3,8,128]{4,3,2,1,0:T(8,128)S(1)} %copy.9), channel_id=1, source_target_pairs={{1,0},{2,1},{3,2},{4,3},{5,4},{6,5},{7,6},{8,7},{9,8},{10,9},{11,1... | collective-permute-start | bytes 2985992 | tf_op jit(solution)/shard_map/ppermute | solution.py:20
Sparse Core Ops, SparseCore 0:
  29.1 113.1 all-reduce.1
where the time goes:
time: 232 us; the launch traced here: 231 us
  waiting for transfers between devices  153 us (66%)
  other arithmetic  24.4 us (11%)
  local copies, waits for them, and re-layouts  15.3 us (7%)
  between operations  14.8 us (6%)
  starting transfers between devices  14.7 us (6%)
  matrix products  9 us (4%)
    psum x1, waiting for transfers between devices, shards(): summed = lax.psum(binned(frames, one_hot), 'rev')  113 us
    ppermute x2, waiting for transfers between devices, padded_2(): lax.ppermute(tail, axis, [(i, (i + 1) % count) for i in range(count)])  20.1 us
    unnamed x33, other arithmetic  19.4 us
    ppermute x2, waiting for transfers between devices, padded_2(): lax.ppermute(head, axis, [((i + 1) % count, i) for i in range(count)])  19.1 us
    ppermute x2, starting transfers between devices, padded_2(): lax.ppermute(tail, axis, [(i, (i + 1) % count) for i in range(count)])  10.6 us
    dot_general x1, matrix products, binned(): jnp.einsum('ps,sfxyz->xfpyz', weights, stacked, precision=lax.Precision.H...  9 us
    unnamed x9, local copies, waits for them, and re-layouts  8.58 us
  transfers between devices with their start and end apart: 5, of which 5 were waited for; matrix products, arithmetic and copies ran while one was open for 1% of the time, Pallas kernels for 0%

commit v1 on v0

--- a/solution.py
+++ b/solution.py
@@ -128,7 +128,8 @@
     one_hot = (local_bins[None, :] == jnp.arange(bins_dev, dtype=jnp.int32)[:, None]).astype(
         jnp.float32
     )
-    summed = lax.psum(binned(frames, one_hot), "rev")
+    quotas_define = lambda field: lax.all_gather(field, "rev").sum(axis=0)
+    summed = quotas_define(binned(frames, one_hot))
     owned = lax.dynamic_slice_in_dim(summed, lax.axis_index("rev") * planes, planes, 0)
     return finish_terms(owned)
 

time: 232 us -> 448 us (1.93)
  waiting for transfers between devices: 153 us -> 355 us
  other arithmetic: 24.4 us -> 38.2 us
    all_gather x0 -> x1, waiting for transfers between devices: none -> 316 us  [shards(): quotas_define = lambda field: lax.all_gather(field, 'rev').sum(axis=0)]
    psum x1 -> x0, waiting for transfers between devices: 113 us -> none  [shards(): summed = lax.psum(binned(frames, one_hot), 'rev')]
    reduce_sum x0 -> x1, other arithmetic: none -> 13.8 us  [shards(): quotas_define = lambda field: lax.all_gather(field, 'rev').sum(axis=0)]
where the time goes in v1:
time: 448 us; the launch traced here: 447 us
  waiting for transfers between devices  355 us (79%)
  other arithmetic  38.2 us (9%)
  local copies, waits for them, and re-layouts  15.3 us (3%)
  between operations  14.8 us (3%)
  starting transfers between devices  14.4 us (3%)
  matrix products  8.88 us (2%)
    all_gather x1, waiting for transfers between devices, shards(): quotas_define = lambda field: lax.all_gather(field, 'rev').sum(axis=0)  316 us
    ppermute x2, waiting for transfers between devices, padded_2(): lax.ppermute(tail, axis, [(i, (i + 1) % count) for i in range(count)])  20.1 us
    unnamed x33, other arithmetic  19.4 us
    ppermute x2, waiting for transfers between devices, padded_2(): lax.ppermute(head, axis, [((i + 1) % count, i) for i in range(count)])  19.3 us
    reduce_sum x1, other arithmetic, shards(): quotas_define = lambda field: lax.all_gather(field, 'rev').sum(axis=0)  13.8 us
    ppermute x2, starting transfers between devices, padded_2(): lax.ppermute(tail, axis, [(i, (i + 1) % count) for i in range(count)])  10.6 us
  transfers between devices with their start and end apart: 5, of which 5 were waited for; matrix products, arithmetic and copies ran while one was open for 1% of the time, Pallas kernels for 0%

profile of v1, /device:TPU:31, one launch (start us, length us, event | category | flops | bytes accessed | tf_op | source)
XLA Modules:
  0.0 446.9 jit_solution(11801526400986275288)
XLA Ops:
  7.2 1.0 broadcast_dynamic-update-slice_fusion
  8.2 3.0 copy.19
  11.2 2.8 constant_dynamic-update-slice_fusion
  14.0 0.9 multiply_dynamic-update-slice_fusion.5
  15.0 1.0 multiply_dynamic-update-slice_fusion.4
  16.0 1.0 multiply_dynamic-update-slice_fusion.3
  17.0 0.9 multiply_dynamic-update-slice_fusion.2
  17.9 1.0 multiply_dynamic-update-slice_fusion.1
  18.9 1.0 multiply_dynamic-update-slice_fusion
  20.0 8.9 %convolution_bitcast_fusion = f32[24,10,4,8,128]{4,2,3,0,1:T(4,128)} fusion(f32[8,10,24,8,128]{4,0,3,2,1:T(8,128)} %multiply_dynamic-update-slice_fusion, s32[8]{0:T(128)S(1)} %subtract_bitcast_fusion), kind=kOutput, calls=%fused_computation.2 | convolution fusion | flops 94371872 | bytes 11796512 | tf_op jit(solution)/shard_map/ps,sfxyz->xfpyz/dot_general | solution.py:49
  28.9 315.7 %all-gather.3.cloned.1.call-done = f32[192,10,4,8,128]{4,2,3,0,1:T(4,128)} async-done(((f32[24,10,4,8,128]{4,2,3,0,1:T(4,128)}), f32[192,10,4,8,128]{4,2,3,0,1:T(4,128)}) %all-gather.3.cloned.1.call-update) | async-done | bytes 31457296 | tf_op jit(solution)/shard_map/all_gather | solution.py:131
  344.6 13.8 %reduce_sum.9 = f32[24,10,4,8,128]{4,2,3,0,1:T(4,128)} reduce(f32[8,24,10,4,8,128]{5,3,4,1,0,2:T(4,128)} %bitcast.213, f32[]{:T(128)} %constant.73.clone.1), dimensions={0}, to_apply=%region_0.0 | reduce | flops 6881280 | bytes 35389444 | tf_op jit(solution)/shard_map/reduce_sum | solution.py:131
  358.5 0.8 constant_dynamic-update-slice_fusion.9
  359.3 0.9 constant_dynamic-update-slice_fusion.8
  360.2 0.9 constant_dynamic-update-slice_fusion.7
  361.0 0.9 constant_dynamic-update-slice_fusion.6
  361.9 0.9 constant_dynamic-update-slice_fusion.5
  362.8 0.9 constant_dynamic-update-slice_fusion.4
  363.6 0.9 constant_dynamic-update-slice_fusion.3
  364.5 0.9 constant_dynamic-update-slice_fusion.2
  365.3 0.9 constant_dynamic-update-slice_fusion.1
  366.2 4.2 collective-permute-start
  370.4 1.9 collective-permute-start.1
  373.9 5.1 %collective-permute-done = f32[3,9,4,8,128]{4,2,3,0,1:T(4,128)S(1)} collective-permute-done((f32[3,9,4,8,128]{4,2,3,0,1:T(4,128)S(1)}, f32[3,9,4,8,128]{4,2,3,0,1:T(4,128)S(1)}, u32[]{:S(2)}, u32[]{:S(2)}) %collective-permute-start) | collective-permute-done | bytes 442400 | tf_op jit(solution)/shard_map/ppermute | solution.py:18
  379.0 5.9 %collective-permute-done.1 = f32[3,9,4,8,128]{4,2,3,0,1:T(4,128)S(1)} collective-permute-done((f32[3,9,4,8,128]{4,2,3,0,1:T(4,128)S(1)}, f32[3,9,4,8,128]{4,2,3,0,1:T(4,128)S(1)}, u32[]{:S(2)}, u32[]{:S(2)}) %collective-permute-start.1) | collective-permute-done | bytes 442400 | tf_op jit(solution)/shard_map/ppermute | solution.py:20
  385.0 0.3 pad_maximum_fusion.1
  385.3 0.8 fusion.99
  386.2 6.4 %collective-permute-start.2 = (f32[9,9,3,8,128]{4,3,2,1,0:T(8,128)S(1)}, f32[9,9,3,8,128]{4,3,2,1,0:T(8,128)S(1)}, u32[]{:S(2)}, u32[]{:S(2)}) collective-permute-start(f32[9,9,3,8,128]{4,3,2,1,0:T(8,128)S(1)} %copy.9), channel_id=1, source_target_pairs={{0,1},{1,2},{2,3},{3,4},{4,5},{5,6},{6,7},{7,8},{8,9},{9,10},{10,1... | collective-permute-start | bytes 2985992 | tf_op jit(solution)/shard_map/ppermute | solution.py:18
  392.7 1.9 collective-permute-start.3
  394.7 0.7 copy.14
  395.8 15.0 %collective-permute-done.2 = f32[9,9,3,8,128]{4,3,2,1,0:T(8,128)S(1)} collective-permute-done((f32[9,9,3,8,128]{4,3,2,1,0:T(8,128)S(1)}, f32[9,9,3,8,128]{4,3,2,1,0:T(8,128)S(1)}, u32[]{:S(2)}, u32[]{:S(2)}) %collective-permute-start.2) | collective-permute-done | bytes 995360 | tf_op jit(solution)/shard_map/ppermute | solution.py:18
  410.8 0.4 copy.11
  411.1 13.4 %collective-permute-done.3 = f32[9,9,3,8,128]{4,3,2,1,0:T(8,128)S(1)} collective-permute-done((f32[9,9,3,8,128]{4,3,2,1,0:T(8,128)S(1)}, f32[9,9,3,8,128]{4,3,2,1,0:T(8,128)S(1)}, u32[]{:S(2)}, u32[]{:S(2)}) %collective-permute-start.3) | collective-permute-done | bytes 995360 | tf_op jit(solution)/shard_map/ppermute | solution.py:20
  424.5 0.4 copy.12
  424.9 1.6 pad_maximum_fusion
  426.5 0.7 slice_bitcast_fusion.3
  427.1 1.3 constant_dynamic-update-slice_fusion.27
  429.9 1.3 constant_dynamic-update-slice_fusion.26
  432.1 1.2 constant_dynamic-update-slice_fusion.25
  434.9 0.3 constant_dynamic-update-slice_fusion.20
  435.7 0.3 constant_dynamic-update-slice_fusion.19
  436.4 0.3 constant_dynamic-update-slice_fusion.18
  437.2 0.3 constant_dynamic-update-slice_fusion.17
  437.5 0.3 constant_dynamic-update-slice_fusion.29
  437.9 0.3 constant_dynamic-update-slice_fusion.16
  438.2 0.3 constant_dynamic-update-slice_fusion.28
  438.6 0.4 maximum_bitcast_fusion
  439.0 1.1 copy.13
  (108 shorter events, 6.9 us)
Async XLA Ops:
  7.2 4.1 copy-start
  7.2 337.5 %all-gather.3.cloned.1.call-start = ((), (), s32[]{:S(2)}) async-start(), calls=%async_computation | async-start | bytes 35389440 | tf_op jit(solution)/shard_map/all_gather | solution.py:131
  16.0 4.0 copy-start.1
  366.2 12.8 %collective-permute-start = (f32[3,9,4,8,128]{4,2,3,0,1:T(4,128)S(1)}, f32[3,9,4,8,128]{4,2,3,0,1:T(4,128)S(1)}, u32[]{:S(2)}, u32[]{:S(2)}) collective-permute-start(f32[3,9,4,8,128]{4,2,3,0,1:T(4,128)S(1)} %constant_dynamic-update-slice_fusion.1), channel_id=1, source_target_pairs={{0,64},{64,128},{128,192},{192,256},{256,320},{320,384},{384,448},... | collective-permute-start | bytes 1327112 | tf_op jit(solution)/shard_map/ppermute | solution.py:18
  370.4 14.6 %collective-permute-start.1 = (f32[3,9,4,8,128]{4,2,3,0,1:T(4,128)S(1)}, f32[3,9,4,8,128]{4,2,3,0,1:T(4,128)S(1)}, u32[]{:S(2)}, u32[]{:S(2)}) collective-permute-start(f32[3,9,4,8,128]{4,2,3,0,1:T(4,128)S(1)} %constant_dynamic-update-slice_fusion.1), channel_id=1, source_target_pairs={{64,0},{128,64},{192,128},{256,192},{320,256},{384,320},{448,384},... | collective-permute-start | bytes 1327112 | tf_op jit(solution)/shard_map/ppermute | solution.py:20
  386.2 24.5 %collective-permute-start.2 = (f32[9,9,3,8,128]{4,3,2,1,0:T(8,128)S(1)}, f32[9,9,3,8,128]{4,3,2,1,0:T(8,128)S(1)}, u32[]{:S(2)}, u32[]{:S(2)}) collective-permute-start(f32[9,9,3,8,128]{4,3,2,1,0:T(8,128)S(1)} %copy.9), channel_id=1, source_target_pairs={{0,1},{1,2},{2,3},{3,4},{4,5},{5,6},{6,7},{7,8},{8,9},{9,10},{10,1... | collective-permute-start | bytes 2985992 | tf_op jit(solution)/shard_map/ppermute | solution.py:18
  392.7 31.8 %collective-permute-start.3 = (f32[9,9,3,8,128]{4,3,2,1,0:T(8,128)S(1)}, f32[9,9,3,8,128]{4,3,2,1,0:T(8,128)S(1)}, u32[]{:S(2)}, u32[]{:S(2)}) collective-permute-start(f32[9,9,3,8,128]{4,3,2,1,0:T(8,128)S(1)} %copy.10), channel_id=1, source_target_pairs={{1,0},{2,1},{3,2},{4,3},{5,4},{6,5},{7,6},{8,7},{9,8},{10,9},{11,1... | collective-permute-start | bytes 2985992 | tf_op jit(solution)/shard_map/ppermute | solution.py:20
Sparse Core Ops, SparseCore 0:
  29.0 315.5 all-gather.2
